TPU v7x, 512 devices: a whole 4x8x8 slice. The times are simulated.
512 devices in a mesh: dp: 16 (over y, core), comp: 32 (over z, x).
Axes of the slice: x: 4, y: 8, z: 8, core: 2. Of those that a mesh axis runs over, the one named last changes fastest.
Arguments:
- descriptors: bfloat16 [65536, 256], P('dp'), may hold values from -12 to 12
- means: float32 [16384, 256], P('comp'), may hold values from -3 to 3
- variances: float32 [16384, 256], P('comp'), may hold values from 0.5 to 2
- log_weights: float32 [16384], P('comp'), may hold values from -2 to 2
Outputs:
- new_log_weights: float32 [16384], P('comp')
- new_means: float32 [16384, 256], P('comp')
- new_variances: float32 [16384, 256], P('comp')
All inputs are finite; a program needn't handle non-finite values.
Results may differ from a plain program's by a relative error of at most 0.002.
Values sent between devices are 32-bit elements; how exact they have to be, the bound alone decides.
No kernel may reach another device: no remote copies, remote signals or barrier semaphores. Data moves between devices by JAX's collectives and lax.ppermute only.
A program may use at most 64 MiB of HBM per device.

v0:
```python
import jax
import jax.numpy as jnp
from jax import lax
from jax.sharding import PartitionSpec as P

prior_count = 1.0
log_two_pi = 1.8378770664093453


def finish(moments, counts, means, variances, grand_total):
    feature_width = means.shape[1]
    weight = counts + prior_count
    new_means = (moments[:, :feature_width] + prior_count * means) / weight[:, None]
    new_variances = (
        moments[:, feature_width:] + prior_count * (variances + means * means)
    ) / weight[:, None] - new_means * new_means
    new_log_weights = jnp.log(weight) - jnp.log(grand_total)
    return (new_log_weights, new_means, new_variances)


def on_device(descriptors, means, variances, log_weights):
    row_count = descriptors.shape[0]
    feature_width = descriptors.shape[1]
    owned_count = means.shape[0]
    grand_total = row_count * lax.axis_size("dp") + prior_count * owned_count * lax.axis_size(
        "comp"
    )
    precision = 1.0 / variances
    scaled_means = means * precision
    loading = jnp.concatenate([-0.5 * precision, scaled_means], axis=1)
    offset = log_weights - 0.5 * jnp.sum(
        means * scaled_means + jnp.log(variances) + log_two_pi, axis=1
    )
    block_rows = min(512, row_count)
    stacked = descriptors.reshape(row_count // block_rows, block_rows, feature_width)

    def score_block(row_block):
        exact = row_block.astype(jnp.float32)
        features = jnp.concatenate([exact * exact, exact], axis=1)
        return (
            lax.dot_general(
                features,
                loading,
                (((1,), (1,)), ((), ())),
                precision=lax.Precision.HIGHEST,
                preferred_element_type=jnp.float32,
            )
            + offset[None, :]
        )

    scores = lax.map(score_block, stacked).reshape(row_count, owned_count)
    row_max = lax.pmax(jnp.max(scores, axis=1), "comp")
    row_sum = lax.psum(jnp.sum(jnp.exp(scores - row_max[:, None]), axis=1), "comp")
    log_total = row_max + jnp.log(row_sum)
    responsibility = jnp.exp(scores - log_total[:, None])
    counts = jnp.sum(responsibility, axis=0)
    resp_half = responsibility.astype(jnp.bfloat16)
    exact_rows = descriptors.astype(jnp.float32)
    halves = jnp.concatenate([descriptors, (exact_rows * exact_rows).astype(jnp.bfloat16)], axis=1)
    moments = lax.dot_general(
        resp_half, halves, (((0,), (0,)), ((), ())), preferred_element_type=jnp.float32
    )
    summed_moments, summed_counts = lax.psum((moments, counts), "dp")
    new_log_weights, new_means, new_variances = finish(
        summed_moments, summed_counts, means, variances, grand_total
    )
    return (new_log_weights, new_means, new_variances)


def solution(mesh):
    placed = (P("dp", None), P("comp", None), P("comp", None), P("comp"))
    return jax.shard_map(
        on_device,
        mesh=mesh,
        in_specs=placed,
        out_specs=(P("comp"), P("comp", None), P("comp", None)),
        check_vma=False,
    )
```

profile of v0, /device:TPU:1, one launch (start us, length us, event | category | flops | bytes accessed | tf_op | source)
XLA Modules:
  0.0 460.0 jit_solution(11352308650413129347)
XLA Ops:
  7.2 0.0 copy-start
  7.2 0.0 copy-start.4
  7.2 0.0 all-reduce.2.cloned.1.call-start
  7.2 3.5 multiply_convert_fusion
  10.8 1.5 add_reduce_fusion
  12.2 0.1 pad_maximum_fusion
  12.4 0.0 copy-done.4
  12.4 0.0 copy-done
  12.4 23.7 %while.10 = (s32[]{:T(128)}, f32[8,512,512]{2,1,0:T(8,128)}, bf16[8,512,256]{2,1,0:T(8,128)(2,1)S(1)}, f32[512,512]{1,0:T(8,128)S(1)}, f32[512]{0:T(512)S(1)}, /*index=5*/s32[]{:T(128)}) while((s32[]{:T(128)}, f32[8,512,512]{2,1,0:T(8,128)}, bf16[8,512,256]{2,1,0:T(8,128)(2,1)S(1)}, f32[512,512]{1,0:T(8,128)S(1)}, f32[512]{0:T(512)S(1)}, ...), condition=%wide.region_2.3_spmd, body=%wide.region_1.2_spmd.sunk | while | flops 1611530240 | bytes 4721229 | solution.py:51
  12.5 2.9 fusion.28
  15.5 2.9 fusion.28
  18.5 2.9 fusion.28
  21.4 2.9 fusion.28
  24.4 2.8 fusion.28
  27.3 2.9 fusion.28
  30.3 2.9 fusion.28
  33.3 2.8 fusion.28
  36.1 4.0 reduce_max.11
  40.2 121.8 %pmax.7 = f32[4096]{0:T(1024)S(1)} all-reduce(f32[4096]{0:T(1024)S(1)} %bitcast.34), channel_id=1, replica_groups=mesh['dp'=16,'comp'=32] {'comp'}, use_global_device_ids=true, to_apply=%region_4.5 | all-reduce | flops 4096 | bytes 32768 | tf_op jit(solution)/shard_map/pmax | solution.py:52
  162.0 4.4 exponential_reduce_fusion.1
  166.4 110.4 %psum.21 = f32[4096]{0:T(1024)S(1)} all-reduce(f32[4096]{0:T(1024)S(1)} %bitcast.35), channel_id=1, replica_groups=mesh['dp'=16,'comp'=32] {'comp'}, use_global_device_ids=true, to_apply=%region_6.7 | all-reduce | flops 4096 | bytes 32768 | tf_op jit(solution)/shard_map/psum | solution.py:53
  276.8 0.0 copy-start.1
  276.8 4.2 fusion.8
  281.1 0.0 copy-done.1
  281.1 3.3 fusion.9
  284.4 0.0 copy-start.2
  284.4 0.0 copy-start.3
  284.4 0.0 all-reduce.2.cloned.1.call-update
  284.5 4.2 exponential_reduce_fusion
  288.6 79.3 %psum.22 = f32[512]{0:T(512)S(1)} all-reduce(f32[512]{0:T(512)S(1)} %exponential_reduce_fusion), channel_id=1, replica_groups=mesh['dp'=16,'comp'=32] {'dp'}, use_global_device_ids=true, to_apply=%region_8.9 | all-reduce | flops 512 | bytes 4096 | tf_op jit(solution)/shard_map/psum | solution.py:63
  368.0 0.6 broadcast_add_fusion
  368.6 82.2 %all-reduce.2.cloned.1.call-done = f32[512,512]{1,0:T(8,128)} async-done(((f32[512,512]{1,0:T(8,128)}), f32[512,512]{1,0:T(8,128)}) %all-reduce.2.cloned.1.call-update) | async-done | bytes 1048592 | tf_op jit(solution)/shard_map/psum | solution.py:63
  450.8 0.0 copy-done.2
  450.8 0.0 copy-done.3
  450.8 2.4 fusion.14
  (23 shorter events, 0.7 us)
Async XLA Ops:
  7.2 5.3 %copy-start = (bf16[4096,256]{1,0:T(8,128)(2,1)S(1)}, bf16[4096,256]{1,0:T(8,128)(2,1)}, u32[]{:S(2)}) copy-start(bf16[4096,256]{1,0:T(8,128)(2,1)} %param.6) | copy-start | bytes 6291460
  7.2 5.2 %copy-start.4 = (f32[512]{0:T(512)S(1)}, f32[512]{0:T(512)}, u32[]{:S(2)}) copy-start(f32[512]{0:T(512)} %param.9) | copy-start | bytes 6148
  7.2 443.6 %all-reduce.2.cloned.1.call-start = ((), (), s32[]{:S(2)}) async-start(), calls=%async_computation | async-start | bytes 2097152 | tf_op jit(solution)/shard_map/psum | solution.py:63
  276.8 4.3 copy-start.1
  284.4 166.3 %copy-start.2 = (f32[512,256]{1,0:T(8,128)S(1)}, f32[512,256]{1,0:T(8,128)}, u32[]{:S(2)}) copy-start(f32[512,256]{1,0:T(8,128)} %param.8) | copy-start | bytes 1572868
  284.4 166.3 %copy-start.3 = (f32[512,256]{1,0:T(8,128)S(1)}, f32[512,256]{1,0:T(8,128)}, u32[]{:S(2)}) copy-start(f32[512,256]{1,0:T(8,128)} %param.7) | copy-start | bytes 1572868
Sparse Core Ops, SparseCore 0:
  284.6 166.1 all-reduce.1
where the time goes:
time: 460 us
  blocking collectives  312 us (68%)
  waiting for transfers between devices  82.2 us (18%)
  matrix products  26.3 us (6%)
  other arithmetic  25.6 us (6%)
  between operations  14.1 us (3%)
    pmax x1, blocking collectives, on_device(): row_max = lax.pmax(jnp.max(scores, axis=1), 'comp')  122 us
    psum x1, blocking collectives, on_device(): lax.psum(jnp.sum(jnp.exp(scores - row_max[:, None]), axis=1), 'comp')  110 us
    psum x1, waiting for transfers between devices, on_device(): summed_moments, summed_counts = lax.psum((moments, counts), 'dp')  82.2 us
    psum x1, blocking collectives, on_device(): summed_moments, summed_counts = lax.psum((moments, counts), 'dp')  79.3 us
    dot_general x8, matrix products, score_block(): lax.dot_general(features, loading, (((1,), (1,)), ((), ())), precision=la...  22.9 us
  transfers between devices with their start and end apart: 1, of which 1 were waited for; matrix products, arithmetic and copies ran while one was open for 1% of the time, Pallas kernels for 0%

commit v1 on v0

--- a/solution.py
+++ b/solution.py
@@ -50,7 +50,9 @@
 
     scores = lax.map(score_block, stacked).reshape(row_count, owned_count)
     row_max = lax.pmax(jnp.max(scores, axis=1), "comp")
-    row_sum = lax.psum(jnp.sum(jnp.exp(scores - row_max[:, None]), axis=1), "comp")
+    content = jnp.sum(jnp.exp(scores - row_max[:, None]), axis=1)
+    aux = jax.lax.all_gather(content, axis_name="comp")
+    row_sum = jnp.sum(aux, 0)
     log_total = row_max + jnp.log(row_sum)
     responsibility = jnp.exp(scores - log_total[:, None])
     counts = jnp.sum(responsibility, axis=0)

time: 460 us -> 373 us (0.81)
  blocking collectives: 312 us -> 220 us
    psum x1 -> x0, blocking collectives: 110 us -> none  [on_device(): lax.psum(jnp.sum(jnp.exp(scores - row_max[:, None]), axis=1), 'comp')]
    all_gather x0 -> x1, blocking collectives: none -> 35.1 us  [on_device(): aux = jax.lax.all_gather(content, axis_name='comp')]
    psum x1, blocking collectives: 79.3 us -> 63.1 us  [on_device(): summed_moments, summed_counts = lax.psum((moments, counts), 'dp')]
where the time goes in v1:
time: 373 us; the launch traced here: 372 us
  blocking collectives  220 us (59%)
  waiting for transfers between devices  85.7 us (23%)
  matrix products  26.3 us (7%)
  other arithmetic  25.9 us (7%)
  between operations  14.2 us (4%)
    pmax x1, blocking collectives, on_device(): row_max = lax.pmax(jnp.max(scores, axis=1), 'comp')  122 us
    psum x1, waiting for transfers between devices, on_device(): summed_moments, summed_counts = lax.psum((moments, counts), 'dp')  85.7 us
    psum x1, blocking collectives, on_device(): summed_moments, summed_counts = lax.psum((moments, counts), 'dp')  63.1 us
    all_gather x1, blocking collectives, on_device(): aux = jax.lax.all_gather(content, axis_name='comp')  35.1 us
    dot_general x8, matrix products, score_block(): lax.dot_general(features, loading, (((1,), (1,)), ((), ())), precision=la...  22.9 us
  transfers between devices with their start and end apart: 1, of which 1 were waited for; matrix products, arithmetic and copies ran while one was open for 1% of the time, Pallas kernels for 0%

profile of v1, /device:TPU:1, one launch (start us, length us, event | category | flops | bytes accessed | tf_op | source)
XLA Modules:
  0.0 372.4 jit_solution(17839552868517572873)
XLA Ops:
  7.2 0.0 copy-start
  7.2 0.0 copy-start.4
  7.2 0.0 all-reduce.2.cloned.1.call-start
  7.2 3.5 multiply_convert_fusion
  10.8 1.5 add_reduce_fusion
  12.2 0.1 pad_maximum_fusion
  12.4 0.0 copy-done.4
  12.4 0.0 copy-done
  12.4 23.7 %while.10 = (s32[]{:T(128)}, f32[8,512,512]{2,1,0:T(8,128)}, bf16[8,512,256]{2,1,0:T(8,128)(2,1)S(1)}, f32[512,512]{1,0:T(8,128)S(1)}, f32[512]{0:T(512)S(1)}, /*index=5*/s32[]{:T(128)}) while((s32[]{:T(128)}, f32[8,512,512]{2,1,0:T(8,128)}, bf16[8,512,256]{2,1,0:T(8,128)(2,1)S(1)}, f32[512,512]{1,0:T(8,128)S(1)}, f32[512]{0:T(512)S(1)}, ...), condition=%wide.region_2.3_spmd, body=%wide.region_1.2_spmd.sunk | while | flops 1611530240 | bytes 4721229 | solution.py:51
  12.5 2.9 fusion.28
  15.5 2.9 fusion.28
  18.5 2.9 fusion.28
  21.4 2.9 fusion.28
  24.4 2.8 fusion.28
  27.3 2.9 fusion.28
  30.3 2.9 fusion.28
  33.3 2.8 fusion.28
  36.1 4.0 %reduce_max.11 = f32[8,512]{1,0:T(8,128)S(1)} reduce(f32[8,512,512]{2,1,0:T(8,128)} %get-tuple-element.30, f32[]{:T(128)} %constant.10.clone.1), dimensions={2}, to_apply=%region_3.4 | reduce | flops 2093056 | bytes 8404996 | tf_op jit(solution)/shard_map/reduce_max | solution.py:52
  40.2 121.8 %pmax.7 = f32[4096]{0:T(1024)S(1)} all-reduce(f32[4096]{0:T(1024)S(1)} %bitcast.31), channel_id=1, replica_groups=mesh['dp'=16,'comp'=32] {'comp'}, use_global_device_ids=true, to_apply=%region_4.5 | all-reduce | flops 4096 | bytes 32768 | tf_op jit(solution)/shard_map/pmax | solution.py:52
  162.0 4.4 %exponential_reduce_fusion.1 = f32[8,512]{1,0:T(8,128)S(1)} fusion(f32[8,512,512]{2,1,0:T(8,128)} %get-tuple-element.30, f32[8,512]{1,0:T(8,128)S(1)} %sub.37), kind=kLoop, calls=%fused_computation.13 | loop fusion | flops 4190208 | bytes 8421376 | tf_op jit(solution)/shard_map/reduce_sum | solution.py:53
  166.4 35.1 %all-gather = f32[32,1,4096]{2,1,0:T(1,128)S(1)} all-gather(f32[1,1,4096]{2,1,0:T(1,128)S(1)} %reshape.34), channel_id=1, replica_groups=mesh['dp'=16,'comp'=32] {'comp'}, dimensions={0}, use_global_device_ids=true | all-gather | bytes 540672 | tf_op jit(solution)/shard_map/all_gather | solution.py:54
  201.6 0.4 reduce_sum.38
  201.9 0.0 copy-start.1
  201.9 4.2 %fusion.8 = bf16[4096,512]{1,0:T(8,128)(2,1)S(1)} fusion(f32[8,512,512]{2,1,0:T(8,128)} %get-tuple-element.30, f32[4096]{0:T(1024)S(1)} %log_add_fusion), kind=kLoop, calls=%fused_computation.11 | loop fusion | flops 4194304 | bytes 12599296 | tf_op jit(solution)/shard_map/convert_element_type | solution.py:59
  206.2 0.0 copy-done.1
  206.2 3.3 fusion.9
  209.5 0.0 copy-start.2
  209.5 0.0 copy-start.3
  209.5 0.0 all-reduce.2.cloned.1.call-update
  209.6 4.2 %exponential_reduce_fusion = f32[512]{0:T(512)S(1)} fusion(f32[8,512,512]{2,1,0:T(8,128)} %get-tuple-element.30, f32[8,512]{1,0:T(8,128)S(1)} %sub.40), kind=kLoop, calls=%fused_computation.12 | loop fusion | flops 4193792 | bytes 8407040 | tf_op jit(solution)/shard_map/reduce_sum | solution.py:58
  213.7 63.1 %psum.14 = f32[512]{0:T(512)S(1)} all-reduce(f32[512]{0:T(512)S(1)} %exponential_reduce_fusion), channel_id=1, replica_groups=mesh['dp'=16,'comp'=32] {'dp'}, use_global_device_ids=true, to_apply=%region_8.9 | all-reduce | flops 512 | bytes 4096 | tf_op jit(solution)/shard_map/psum | solution.py:65
  276.9 0.6 broadcast_add_fusion
  277.5 85.7 %all-reduce.2.cloned.1.call-done = f32[512,512]{1,0:T(8,128)} async-done(((f32[512,512]{1,0:T(8,128)}), f32[512,512]{1,0:T(8,128)}) %all-reduce.2.cloned.1.call-update) | async-done | bytes 1048592 | tf_op jit(solution)/shard_map/psum | solution.py:65
  363.2 0.0 copy-done.2
  363.2 0.0 copy-done.3
  363.2 2.4 fusion.14
  (23 shorter events, 0.7 us)
Async XLA Ops:
  7.2 5.3 %copy-start = (bf16[4096,256]{1,0:T(8,128)(2,1)S(1)}, bf16[4096,256]{1,0:T(8,128)(2,1)}, u32[]{:S(2)}) copy-start(bf16[4096,256]{1,0:T(8,128)(2,1)} %param.6) | copy-start | bytes 6291460
  7.2 5.2 %copy-start.4 = (f32[512]{0:T(512)S(1)}, f32[512]{0:T(512)}, u32[]{:S(2)}) copy-start(f32[512]{0:T(512)} %param.9) | copy-start | bytes 6148
  7.2 356.0 %all-reduce.2.cloned.1.call-start = ((), (), s32[]{:S(2)}) async-start(), calls=%async_computation | async-start | bytes 2097152 | tf_op jit(solution)/shard_map/psum | solution.py:65
  201.9 4.3 %copy-start.1 = (bf16[4096,256]{1,0:T(8,128)(2,1)S(1)}, bf16[4096,256]{1,0:T(8,128)(2,1)}, u32[]{:S(2)}) copy-start(bf16[4096,256]{1,0:T(8,128)(2,1)} %multiply_convert_fusion) | copy-start | bytes 6291460
  209.5 153.7 %copy-start.2 = (f32[512,256]{1,0:T(8,128)S(1)}, f32[512,256]{1,0:T(8,128)}, u32[]{:S(2)}) copy-start(f32[512,256]{1,0:T(8,128)} %param.8) | copy-start | bytes 1572868
  209.5 153.7 %copy-start.3 = (f32[512,256]{1,0:T(8,128)S(1)}, f32[512,256]{1,0:T(8,128)}, u32[]{:S(2)}) copy-start(f32[512,256]{1,0:T(8,128)} %param.7) | copy-start | bytes 1572868
Sparse Core Ops, SparseCore 0:
  209.7 153.4 all-reduce.1
